TPU v7x, 128 devices: a whole 4x4x4 slice. The times are simulated.
128 devices in a mesh: row: 4 (over z), col: 32 (over x, y, core).
Axes of the slice: x: 4, y: 4, z: 4, core: 2. Of those that a mesh axis runs over, the one named last changes fastest.
Arguments:
- matrix_real: bfloat16 [512, 16384], P('col', 'row'), may hold values from -0.25 to 0.25
- matrix_imag: bfloat16 [512, 16384], P('col', 'row'), may hold values from -0.25 to 0.25
- valence_index: int32 [512], P('col'), may hold values from 0 to 15
- conduction_index: int32 [512], P('col'), may hold values from 0 to 31
- valence_energy: float32 [16], replicated, may hold values from -1.5 to -0.1
- conduction_energy: float32 [32], replicated, may hold values from 0.1 to 2
- frequency: float32 [2], replicated, may hold values from 0.2 to 2
Outputs:
- chi_real: bfloat16 [2, 16384, 16384], P(None, 'row', 'col')
- chi_imag: bfloat16 [2, 16384, 16384], P(None, 'row', 'col')
All inputs are finite; a program needn't handle non-finite values.
Results may differ from a plain program's by a relative error of at most 0.005.
Values may be sent and summed in bfloat16 or wider, within the bound.
No kernel may reach another device: no remote copies, remote signals or barrier semaphores. Data moves between devices by JAX's collectives and lax.ppermute only.
A program may use at most 192 MiB of HBM per device.

v0:
```python
import jax
import jax.numpy as jnp
from jax import lax
from jax.sharding import PartitionSpec as P


def lookup(indices, table):
    count = table.shape[0]
    picks = indices[:, None] == lax.broadcasted_iota(jnp.int32, (1, count), 1)
    return jnp.sum(jnp.where(picks, table[None, :], 0.0), axis=1)


def contract(left_side, right_side):
    return lax.dot_general(
        left_side, right_side, (((0,), (0,)), ((), ())), preferred_element_type=jnp.float32
    )


def on_device(
    matrix_real,
    matrix_imag,
    valence_index,
    conduction_index,
    valence_energy,
    conduction_energy,
    frequency,
):
    all_valence, all_conduction = (
        lax.all_gather(valence_index, "col", axis=0, tiled=True),
        lax.all_gather(conduction_index, "col", axis=0, tiled=True),
    )
    gap = lookup(all_conduction, conduction_energy) - lookup(all_valence, valence_energy)
    spread_real, spread_imag = (
        lax.all_gather(matrix_real, "row", axis=1, tiled=True),
        lax.all_gather(matrix_imag, "row", axis=1, tiled=True),
    )
    column_real, column_imag = (
        lax.all_to_all(spread_real, "col", split_axis=1, concat_axis=0, tiled=True),
        lax.all_to_all(spread_imag, "col", split_axis=1, concat_axis=0, tiled=True),
    )
    width = column_real.shape[1]
    wide_real = column_real.astype(jnp.float32)
    wide_imag = column_imag.astype(jnp.float32)
    upper_parts = []
    lower_parts = []
    for index in range(frequency.shape[0]):
        omega = frequency[index]
        weight = 4.0 * gap / (gap * gap + omega * omega)
        scaled_real = (weight[:, None] * wide_real).astype(jnp.bfloat16)
        scaled_imag = (weight[:, None] * wide_imag).astype(jnp.bfloat16)
        upper_parts.extend([scaled_real, scaled_imag])
        lower_parts.extend([scaled_imag, -scaled_real])
    upper_side = jnp.concatenate(upper_parts, axis=1)
    lower_side = jnp.concatenate(lower_parts, axis=1)
    right_side = jnp.concatenate([upper_side, lower_side], axis=0)
    block_real, block_imag = (
        lax.all_to_all(matrix_real, "col", split_axis=1, concat_axis=0, tiled=True),
        lax.all_to_all(matrix_imag, "col", split_axis=1, concat_axis=0, tiled=True),
    )
    stacked = jnp.concatenate([block_real, block_imag], axis=0)
    joined = contract(lax.all_gather(stacked, "col", axis=1, tiled=True), right_side)
    real_out = []
    imag_out = []
    for index in range(frequency.shape[0]):
        start = 2 * width * index
        real_out.append((-joined[:, start : start + width]).astype(jnp.bfloat16))
        imag_out.append((-joined[:, start + width : start + 2 * width]).astype(jnp.bfloat16))
    return (jnp.stack(real_out, axis=0), jnp.stack(imag_out, axis=0))


def solution(mesh):
    placed = (P("col", "row"), P("col", "row"), P("col"), P("col"), P(), P(), P())
    return jax.shard_map(
        on_device,
        mesh=mesh,
        in_specs=placed,
        out_specs=(P(None, "row", "col"), P(None, "row", "col")),
        check_vma=False,
    )
```

profile of v0, /device:TPU:1, one launch (start us, length us, event | category | flops | bytes accessed | tf_op | source)
XLA Modules:
  0.0 199.1 jit_solution(13468990475961677798)
XLA Ops:
  7.2 1.6 copy_bitcast_fusion.3
  8.7 8.6 %all-to-all-start = ((bf16[16,32,128]{2,0,1:T(8,128)(2,1)}), bf16[16,32,128]{2,0,1:T(8,128)(2,1)S(1)}, u32[]{:S(2)}, u32[]{:S(2)}) async-start(bf16[16,32,128]{2,0,1:T(8,128)(2,1)} %copy_bitcast_fusion.3), calls=%async_computation | async-start | bytes 262144 | tf_op jit(solution)/shard_map/all_to_all | solution.py:57
  17.3 0.0 all-gather.2.cloned.1.call-start
  17.4 0.9 copy_bitcast_fusion.2
  18.3 6.7 %all-to-all-done = bf16[16,32,128]{2,0,1:T(8,128)(2,1)S(1)} async-done(((bf16[16,32,128]{2,0,1:T(8,128)(2,1)}), bf16[16,32,128]{2,0,1:T(8,128)(2,1)S(1)}, u32[]{:S(2)}, u32[]{:S(2)}) %all-to-all-start) | async-done | bytes 131104 | tf_op jit(solution)/shard_map/all_to_all | solution.py:57
  25.0 11.3 %all_to_all.64 = bf16[16,32,128]{2,0,1:T(8,128)(2,1)S(1)} all-to-all(bf16[16,32,128]{2,0,1:T(8,128)(2,1)S(1)} %copy_bitcast_fusion.2), channel_id=1, replica_groups=mesh['row'=4,'col'=32] {'col'}, dimensions={1} | all-to-all | bytes 262144 | tf_op jit(solution)/shard_map/all_to_all | solution.py:58
  36.3 0.7 pad_maximum_fusion.2
  37.0 0.0 all-gather.2.cloned.1.call-update
  37.1 12.7 %all_gather.19 = bf16[16,16384]{1,0:T(8,128)(2,1)S(1)} all-gather(bf16[16,4096]{1,0:T(8,128)(2,1)} %param.8), channel_id=1, replica_groups=mesh['row'=4,'col'=32] {'row'}, dimensions={1}, use_global_device_ids=true | all-gather | bytes 655360 | tf_op jit(solution)/shard_map/all_gather | solution.py:35
  49.7 0.9 copy.29
  50.6 5.5 %all-to-all-start.3 = ((bf16[16,32,512]{2,0,1:T(8,128)(2,1)}), bf16[16,32,512]{2,0,1:T(8,128)(2,1)S(1)}, u32[]{:S(2)}, u32[]{:S(2)}) async-start(bf16[16,32,512]{2,0,1:T(8,128)(2,1)} %bitcast.54), calls=%async_computation.3 | async-start | bytes 1048576 | tf_op jit(solution)/shard_map/all_to_all | solution.py:39
  56.1 12.0 %all_gather.18 = bf16[16,16384]{1,0:T(8,128)(2,1)S(1)} all-gather(bf16[16,4096]{1,0:T(8,128)(2,1)} %param.7), channel_id=1, replica_groups=mesh['row'=4,'col'=32] {'row'}, dimensions={1}, use_global_device_ids=true | all-gather | bytes 655360 | tf_op jit(solution)/shard_map/all_gather | solution.py:34
  68.1 0.9 copy.30
  68.9 1.3 dynamic-slice
  70.8 0.9 dynamic-update-slice
  71.7 0.9 dynamic-update-slice.1
  72.5 15.7 %all-reduce.2 = (s32[512]{0:T(512)S(1)}, s32[512]{0:T(512)S(1)}) all-reduce(s32[512]{0:T(512)S(1)} %dynamic-update-slice, s32[512]{0:T(512)S(1)} %dynamic-update-slice.1), channel_id=1, replica_groups=mesh['row'=4,'col'=32] {'col'}, use_global_device_ids=true, to_apply=%add | all-reduce | flops 1024 | bytes 8192
  88.3 0.7 select_reduce_fusion.1
  89.0 0.7 select_reduce_fusion
  89.8 0.0 all-to-all-done.3
  89.8 6.8 %all-to-all-start.2 = ((bf16[16,32,512]{2,0,1:T(8,128)(2,1)}), bf16[16,32,512]{2,0,1:T(8,128)(2,1)S(1)}, u32[]{:S(2)}, u32[]{:S(2)}) async-start(bf16[16,32,512]{2,0,1:T(8,128)(2,1)} %bitcast.55), calls=%async_computation.2 | async-start | bytes 1048576 | tf_op jit(solution)/shard_map/all_to_all | solution.py:38
  96.6 1.3 fusion.33
  100.5 0.2 fusion.24
  100.7 7.6 %all-to-all-done.2 = bf16[16,32,512]{2,0,1:T(8,128)(2,1)S(1)} async-done(((bf16[16,32,512]{2,0,1:T(8,128)(2,1)}), bf16[16,32,512]{2,0,1:T(8,128)(2,1)S(1)}, u32[]{:S(2)}, u32[]{:S(2)}) %all-to-all-start.2) | async-done | bytes 524320 | tf_op jit(solution)/shard_map/all_to_all | solution.py:38
  108.3 1.1 fusion.29
  109.4 0.0 all-gather.2.cloned.1.call-done
  109.4 52.4 %fusion.8 = f32[4096,2048]{1,0:T(8,128)} fusion(bf16[1024,4096]{1,0:T(8,128)(2,1)} %all-gather.2.cloned.1.call-done, bf16[512,512]{1,0:T(8,128)(2,1)S(1)} %get-tuple-element.14, bf16[512,512]{1,0:T(8,128)(2,1)S(1)} %get-tuple-element.13, bf16[512,512]{1,0:T(8,128)(2,1)S(1)} %get-tuple-element.4, bf16[512,512]{1,0:T(8,128)(2,1)S(1)} %get-tuple-element.12, ...), kind=kOutput, calls=%fused_computation.14 | convolution fusion | flops 17213423616 | bytes 45088768 | tf_op jit(solution)/shard_map/dot_general | solution.py:14
  161.8 18.9 %fusion.6 = (bf16[1,4096,512]{2,1,0:T(8,128)(2,1)}, bf16[1,4096,512]{2,1,0:T(8,128)(2,1)}, bf16[1,4096,512]{2,1,0:T(8,128)(2,1)}, bf16[1,4096,512]{2,1,0:T(8,128)(2,1)}) fusion(f32[4096,2048]{1,0:T(8,128)} %fusion.8), kind=kLoop, calls=%fused_computation.12 | loop fusion | flops 16777216 | bytes 50331648 | tf_op jit(solution)/shard_map/stack | solution.py:68
  180.7 11.5 %pad_maximum_fusion = (bf16[2,4096,512]{2,1,0:T(8,128)(2,1)}, bf16[2,4096,512]{2,1,0:T(8,128)(2,1)}) fusion(bf16[1,4096,512]{2,1,0:T(8,128)(2,1)} %get-tuple-element.10, bf16[1,4096,512]{2,1,0:T(8,128)(2,1)} %get-tuple-element.11, bf16[1,4096,512]{2,1,0:T(8,128)(2,1)} %get-tuple-element.9, bf16[1,4096,512]{2,1,0:T(8,128)(2,1)} %get-tuple-element.8), kind=kLoop, calls=%fused_computation.8 | loop fusion | flops 8388608 | bytes 33554432 | tf_op jit(solution)/shard_map/stack | solution.py:68
  (3 shorter events, 0.0 us)
Async XLA Ops:
  8.7 16.3 %all-to-all-start = ((bf16[16,32,128]{2,0,1:T(8,128)(2,1)}), bf16[16,32,128]{2,0,1:T(8,128)(2,1)S(1)}, u32[]{:S(2)}, u32[]{:S(2)}) async-start(bf16[16,32,128]{2,0,1:T(8,128)(2,1)} %copy_bitcast_fusion.3), calls=%async_computation | async-start | bytes 262144 | tf_op jit(solution)/shard_map/all_to_all | solution.py:57
  17.3 92.1 %all-gather.2.cloned.1.call-start = ((), (), s32[]{:S(2)}) async-start(), calls=%async_computation.4 | async-start | bytes 8650752 | tf_op jit(solution)/shard_map/all_gather | solution.py:61
  50.6 39.2 %all-to-all-start.3 = ((bf16[16,32,512]{2,0,1:T(8,128)(2,1)}), bf16[16,32,512]{2,0,1:T(8,128)(2,1)S(1)}, u32[]{:S(2)}, u32[]{:S(2)}) async-start(bf16[16,32,512]{2,0,1:T(8,128)(2,1)} %bitcast.54), calls=%async_computation.3 | async-start | bytes 1048576 | tf_op jit(solution)/shard_map/all_to_all | solution.py:39
  89.8 18.5 %all-to-all-start.2 = ((bf16[16,32,512]{2,0,1:T(8,128)(2,1)}), bf16[16,32,512]{2,0,1:T(8,128)(2,1)S(1)}, u32[]{:S(2)}, u32[]{:S(2)}) async-start(bf16[16,32,512]{2,0,1:T(8,128)(2,1)} %bitcast.55), calls=%async_computation.2 | async-start | bytes 1048576 | tf_op jit(solution)/shard_map/all_to_all | solution.py:38
Sparse Core Ops, SparseCore 0:
  37.2 62.9 all-gather.1
where the time goes:
time: 200 us; the launch traced here: 199 us
  matrix products  52.4 us (26%)
  blocking collectives  51.7 us (26%)
  other arithmetic  34 us (17%)
  starting transfers between devices  20.9 us (10%)
  between operations  17.3 us (9%)
  waiting for transfers between devices  14.3 us (7%)
  local copies, waits for them, and re-layouts  8.55 us (4%)
    dot_general x1, matrix products, contract(): lax.dot_general(left_side, right_side, (((0,), (0,)), ((), ())), preferre...  52.4 us
    another operation x2, other arithmetic, on_device(): return (jnp.stack(real_out, axis=0), jnp.stack(imag_out, axis=0))  30.5 us
    unnamed x1, blocking collectives  15.7 us
    all_gather x1, blocking collectives, on_device(): lax.all_gather(matrix_imag, 'row', axis=1, tiled=True)  12.7 us
    all_gather x1, blocking collectives, on_device(): lax.all_gather(matrix_real, 'row', axis=1, tiled=True)  12 us
    all_to_all x1, blocking collectives, on_device(): lax.all_to_all(matrix_imag, 'col', split_axis=1, concat_axis=0, tiled=True)  11.3 us
    all_to_all x1, starting transfers between devices, on_device(): lax.all_to_all(matrix_real, 'col', split_axis=1, concat_axis=0, tiled=True)  8.59 us
    all_to_all x1, waiting for transfers between devices, on_device(): lax.all_to_all(spread_real, 'col', split_axis=1, concat_axis=0, tiled=True)  7.6 us
  transfers between devices with their start and end apart: 4, of which 2 were waited for; matrix products, arithmetic and copies ran while one was open for 5% of the time, Pallas kernels for 0%

commit v1 on v0

--- a/solution.py
+++ b/solution.py
@@ -2,6 +2,28 @@
 import jax.numpy as jnp
 from jax import lax
 from jax.sharding import PartitionSpec as P
+
+
+def laid_out(parts, dim):
+    shape = list(parts.shape[1:])
+    shape[dim] *= parts.shape[0]
+    return jnp.moveaxis(parts, 0, dim).reshape(shape)
+
+
+def gather_around(value, axis, dim):
+    length = lax.axis_size(axis)
+    pairs = [(i, (i + 1) % length) for i in range(length)]
+    back = [(b, a) for a, b in pairs]
+    lower, upper = ([], [])
+    for step in range(length - 1):
+        if step % 2 == 0:
+            lower.append(lax.ppermute(lower[-1] if lower else value, axis, pairs))
+        else:
+            upper.append(lax.ppermute(upper[-1] if upper else value, axis, back))
+    blocks = jnp.stack([*lower[::-1], value, *upper])
+    shift = lax.axis_index(axis) - len(lower)
+    blocks = blocks[(jnp.arange(length) - shift) % length]
+    return laid_out(blocks, dim)
 
 
 def lookup(indices, table):
@@ -31,7 +53,7 @@
     )
     gap = lookup(all_conduction, conduction_energy) - lookup(all_valence, valence_energy)
     spread_real, spread_imag = (
-        lax.all_gather(matrix_real, "row", axis=1, tiled=True),
+        gather_around(matrix_real, "row", 1),
         lax.all_gather(matrix_imag, "row", axis=1, tiled=True),
     )
     column_real, column_imag = (

time: 200 us -> 198 us (0.990)
  blocking collectives: 51.7 us -> 36.5 us
  starting transfers between devices: 20.9 us -> 27.3 us
  waiting for transfers between devices: 14.3 us -> 19.7 us
    all_gather x1 -> x0, blocking collectives: 12 us -> none  [on_device(): lax.all_gather(matrix_real, 'row', axis=1, tiled=True)]
    ppermute x0 -> x3, starting transfers between devices: none -> 4.87 us  [the longest x2 2.67 us: gather_around(): lower.append(lax.ppermute(lower[-1] if lower else value, axis, pairs))]
    ppermute x0 -> x3, waiting for transfers between devices: none -> 4.51 us  [the longest x2 4.5 us: gather_around(): lower.append(lax.ppermute(lower[-1] if lower else value, axis, pairs))]
  transfers between devices with their start and end apart: 4 -> 7, of which waited for: 2 -> 3; matrix products, arithmetic and copies ran while one was open for 5% -> 6% of each run, Pallas kernels for 0% -> 0%
where the time goes in v1:
time: 198 us; the launch traced here: 197 us
  matrix products  52.4 us (26%)
  blocking collectives  36.5 us (18%)
  other arithmetic  35 us (18%)
  starting transfers between devices  27.3 us (14%)
  waiting for transfers between devices  19.7 us (10%)
  between operations  17.2 us (9%)
  local copies, waits for them, and re-layouts  9.36 us (5%)
    dot_general x1, matrix products, contract(): lax.dot_general(left_side, right_side, (((0,), (0,)), ((), ())), preferre...  52.4 us
    another operation x2, other arithmetic, on_device(): return (jnp.stack(real_out, axis=0), jnp.stack(imag_out, axis=0))  30.5 us
    unnamed x1, blocking collectives  14.2 us
    all_to_all x1, blocking collectives, on_device(): lax.all_to_all(matrix_real, 'col', split_axis=1, concat_axis=0, tiled=True)  11.3 us
    all_gather x1, blocking collectives, on_device(): lax.all_gather(matrix_imag, 'row', axis=1, tiled=True)  11 us
    all_to_all x1, starting transfers between devices, on_device(): lax.all_to_all(matrix_imag, 'col', split_axis=1, concat_axis=0, tiled=True)  8.59 us
    all_to_all x1, waiting for transfers between devices, on_device(): lax.all_to_all(spread_real, 'col', split_axis=1, concat_axis=0, tiled=True)  8.47 us
    all_to_all x1, starting transfers between devices, on_device(): lax.all_to_all(spread_real, 'col', split_axis=1, concat_axis=0, tiled=True)  7.23 us
  transfers between devices with their start and end apart: 7, of which 3 were waited for; matrix products, arithmetic and copies ran while one was open for 6% of the time, Pallas kernels for 0%

profile of v1, /device:TPU:1, one launch (start us, length us, event | category | flops | bytes accessed | tf_op | source)
XLA Modules:
  0.0 197.5 jit_solution(8751221792656040309)
XLA Ops:
  7.2 0.0 copy-start
  7.2 1.6 copy_bitcast_fusion.1
  8.8 8.6 %all-to-all-start.1 = ((bf16[16,32,128]{2,0,1:T(8,128)(2,1)}), bf16[16,32,128]{2,0,1:T(8,128)(2,1)S(1)}, u32[]{:S(2)}, u32[]{:S(2)}) async-start(bf16[16,32,128]{2,0,1:T(8,128)(2,1)} %copy_bitcast_fusion.1), calls=%async_computation.1 | async-start | bytes 262144 | tf_op jit(solution)/shard_map/all_to_all | solution.py:80
  17.4 0.0 all-gather.2.cloned.1.call-start
  17.4 0.9 copy_bitcast_fusion.2
  18.3 6.7 %all-to-all-done.1 = bf16[16,32,128]{2,0,1:T(8,128)(2,1)S(1)} async-done(((bf16[16,32,128]{2,0,1:T(8,128)(2,1)}), bf16[16,32,128]{2,0,1:T(8,128)(2,1)S(1)}, u32[]{:S(2)}, u32[]{:S(2)}) %all-to-all-start.1) | async-done | bytes 131104 | tf_op jit(solution)/shard_map/all_to_all | solution.py:80
  25.1 11.3 %all_to_all.64 = bf16[16,32,128]{2,0,1:T(8,128)(2,1)S(1)} all-to-all(bf16[16,32,128]{2,0,1:T(8,128)(2,1)S(1)} %copy_bitcast_fusion.2), channel_id=1, replica_groups=mesh['row'=4,'col'=32] {'col'}, dimensions={1} | all-to-all | bytes 262144 | tf_op jit(solution)/shard_map/all_to_all | solution.py:79
  36.3 0.7 pad_maximum_fusion.3
  37.1 0.0 all-gather.2.cloned.1.call-update
  37.1 1.7 collective-permute-start
  38.8 2.2 %collective-permute-start.2 = (bf16[16,4096]{1,0:T(8,128)(2,1)}, bf16[16,4096]{1,0:T(8,128)(2,1)S(1)}, u32[]{:S(2)}, u32[]{:S(2)}) collective-permute-start(bf16[16,4096]{1,0:T(8,128)(2,1)} %param.7), channel_id=1, source_target_pairs={{32,0},{64,32},{96,64},{0,96},{33,1},{65,33},{97,65},{1,97},{34,2}... | collective-permute-start | bytes 393224 | tf_op jit(solution)/shard_map/ppermute | solution.py:22
  41.0 11.0 %all_gather.15 = bf16[16,16384]{1,0:T(8,128)(2,1)S(1)} all-gather(bf16[16,4096]{1,0:T(8,128)(2,1)} %param.8), channel_id=1, replica_groups=mesh['row'=4,'col'=32] {'row'}, dimensions={1}, use_global_device_ids=true | all-gather | bytes 655360 | tf_op jit(solution)/shard_map/all_gather | solution.py:57
  52.0 0.9 copy.31
  52.8 6.6 %all-to-all-start.3 = ((bf16[16,32,512]{2,0,1:T(8,128)(2,1)}), bf16[16,32,512]{2,0,1:T(8,128)(2,1)S(1)}, u32[]{:S(2)}, u32[]{:S(2)}) async-start(bf16[16,32,512]{2,0,1:T(8,128)(2,1)} %bitcast.58), calls=%async_computation.3 | async-start | bytes 1048576 | tf_op jit(solution)/shard_map/all_to_all | solution.py:61
  59.4 1.2 dynamic-slice
  61.3 0.9 dynamic-update-slice
  62.2 0.8 dynamic-update-slice.1
  63.0 14.2 %all-reduce.2 = (s32[512]{0:T(512)S(1)}, s32[512]{0:T(512)S(1)}) all-reduce(s32[512]{0:T(512)S(1)} %dynamic-update-slice, s32[512]{0:T(512)S(1)} %dynamic-update-slice.1), channel_id=1, replica_groups=mesh['row'=4,'col'=32] {'col'}, use_global_device_ids=true, to_apply=%add | all-reduce | flops 1024 | bytes 8192
  77.3 0.8 select_reduce_fusion.1
  78.0 0.7 select_reduce_fusion
  78.8 0.0 collective-permute-done
  78.8 1.0 collective-permute-start.1
  79.8 0.0 collective-permute-done.2
  79.8 4.5 %collective-permute-done.1 = bf16[16,4096]{1,0:T(8,128)(2,1)S(1)} collective-permute-done((bf16[16,4096]{1,0:T(8,128)(2,1)S(1)}, bf16[16,4096]{1,0:T(8,128)(2,1)S(1)}, u32[]{:S(2)}, u32[]{:S(2)}) %collective-permute-start.1) | collective-permute-done | bytes 131104 | tf_op jit(solution)/shard_map/ppermute | solution.py:20
  84.3 1.0 pad_maximum_fusion.2
  85.3 0.6 gather_fusion
  85.8 0.4 copy.22
  86.3 0.4 all_to_all.56
  86.6 1.1 copy.23
  87.7 0.0 all-to-all-done.3
  87.7 7.2 %all-to-all-start.2 = ((bf16[16,32,512]{2,0,1:T(8,128)(2,1)}), bf16[16,32,512]{2,0,1:T(8,128)(2,1)S(1)}, u32[]{:S(2)}, u32[]{:S(2)}) async-start(bf16[16,32,512]{2,0,1:T(8,128)(2,1)} %copy.23), calls=%async_computation.2 | async-start | bytes 1048576 | tf_op jit(solution)/shard_map/all_to_all | solution.py:60
  95.0 0.0 copy-done
  95.0 0.6 fusion.35
  98.0 0.2 fusion.24
  98.2 8.5 %all-to-all-done.2 = bf16[16,32,512]{2,0,1:T(8,128)(2,1)S(1)} async-done(((bf16[16,32,512]{2,0,1:T(8,128)(2,1)}), bf16[16,32,512]{2,0,1:T(8,128)(2,1)S(1)}, u32[]{:S(2)}, u32[]{:S(2)}) %all-to-all-start.2) | async-done | bytes 524320 | tf_op jit(solution)/shard_map/all_to_all | solution.py:60
  106.7 1.1 fusion.31
  107.8 0.0 all-gather.2.cloned.1.call-done
  107.8 52.4 %fusion.8 = f32[4096,2048]{1,0:T(8,128)} fusion(bf16[1024,4096]{1,0:T(8,128)(2,1)} %all-gather.2.cloned.1.call-done, bf16[512,512]{1,0:T(8,128)(2,1)S(1)} %get-tuple-element.14, bf16[512,512]{1,0:T(8,128)(2,1)S(1)} %get-tuple-element.13, bf16[512,512]{1,0:T(8,128)(2,1)S(1)} %get-tuple-element.4, bf16[512,512]{1,0:T(8,128)(2,1)S(1)} %get-tuple-element.12, ...), kind=kOutput, calls=%fused_computation.15 | convolution fusion | flops 17213423616 | bytes 45088768 | tf_op jit(solution)/shard_map/dot_general | solution.py:36
  160.2 18.9 %fusion.6 = (bf16[1,4096,512]{2,1,0:T(8,128)(2,1)}, bf16[1,4096,512]{2,1,0:T(8,128)(2,1)}, bf16[1,4096,512]{2,1,0:T(8,128)(2,1)}, bf16[1,4096,512]{2,1,0:T(8,128)(2,1)}) fusion(f32[4096,2048]{1,0:T(8,128)} %fusion.8), kind=kLoop, calls=%fused_computation.13 | loop fusion | flops 16777216 | bytes 50331648 | tf_op jit(solution)/shard_map/stack | solution.py:90
  179.1 11.5 %pad_maximum_fusion = (bf16[2,4096,512]{2,1,0:T(8,128)(2,1)}, bf16[2,4096,512]{2,1,0:T(8,128)(2,1)}) fusion(bf16[1,4096,512]{2,1,0:T(8,128)(2,1)} %get-tuple-element.10, bf16[1,4096,512]{2,1,0:T(8,128)(2,1)} %get-tuple-element.11, bf16[1,4096,512]{2,1,0:T(8,128)(2,1)} %get-tuple-element.9, bf16[1,4096,512]{2,1,0:T(8,128)(2,1)} %get-tuple-element.8), kind=kLoop, calls=%fused_computation.9 | loop fusion | flops 8388608 | bytes 33554432 | tf_op jit(solution)/shard_map/stack | solution.py:90
  (5 shorter events, 0.0 us)
Async XLA Ops:
  7.2 87.8 %copy-start = (f32[2]{0:T(128)S(1)}, f32[2]{0:T(128)}, u32[]{:S(2)}) copy-start(f32[2]{0:T(128)} %param.13) | copy-start | bytes 28
  8.8 16.3 %all-to-all-start.1 = ((bf16[16,32,128]{2,0,1:T(8,128)(2,1)}), bf16[16,32,128]{2,0,1:T(8,128)(2,1)S(1)}, u32[]{:S(2)}, u32[]{:S(2)}) async-start(bf16[16,32,128]{2,0,1:T(8,128)(2,1)} %copy_bitcast_fusion.1), calls=%async_computation.1 | async-start | bytes 262144 | tf_op jit(solution)/shard_map/all_to_all | solution.py:80
  17.4 90.5 %all-gather.2.cloned.1.call-start = ((), (), s32[]{:S(2)}) async-start(), calls=%async_computation.4 | async-start | bytes 8650752 | tf_op jit(solution)/shard_map/all_gather | solution.py:83
  37.1 41.7 %collective-permute-start = (bf16[16,4096]{1,0:T(8,128)(2,1)}, bf16[16,4096]{1,0:T(8,128)(2,1)S(1)}, u32[]{:S(2)}, u32[]{:S(2)}) collective-permute-start(bf16[16,4096]{1,0:T(8,128)(2,1)} %param.7), channel_id=1, source_target_pairs={{0,32},{32,64},{64,96},{96,0},{1,33},{33,65},{65,97},{97,1},{2,34}... | collective-permute-start | bytes 393224 | tf_op jit(solution)/shard_map/ppermute | solution.py:20
  38.8 41.0 %collective-permute-start.2 = (bf16[16,4096]{1,0:T(8,128)(2,1)}, bf16[16,4096]{1,0:T(8,128)(2,1)S(1)}, u32[]{:S(2)}, u32[]{:S(2)}) collective-permute-start(bf16[16,4096]{1,0:T(8,128)(2,1)} %param.7), channel_id=1, source_target_pairs={{32,0},{64,32},{96,64},{0,96},{33,1},{65,33},{97,65},{1,97},{34,2}... | collective-permute-start | bytes 393224 | tf_op jit(solution)/shard_map/ppermute | solution.py:22
  52.8 34.9 %all-to-all-start.3 = ((bf16[16,32,512]{2,0,1:T(8,128)(2,1)}), bf16[16,32,512]{2,0,1:T(8,128)(2,1)S(1)}, u32[]{:S(2)}, u32[]{:S(2)}) async-start(bf16[16,32,512]{2,0,1:T(8,128)(2,1)} %bitcast.58), calls=%async_computation.3 | async-start | bytes 1048576 | tf_op jit(solution)/shard_map/all_to_all | solution.py:61
  78.8 5.5 %collective-permute-start.1 = (bf16[16,4096]{1,0:T(8,128)(2,1)S(1)}, bf16[16,4096]{1,0:T(8,128)(2,1)S(1)}, u32[]{:S(2)}, u32[]{:S(2)}) collective-permute-start(bf16[16,4096]{1,0:T(8,128)(2,1)S(1)} %collective-permute-done), channel_id=1, source_target_pairs={{0,32},{32,64},{64,96},{96,0},{1,33},{33,65},{65,97},{97,1},{2,34}... | collective-permute-start | bytes 393224 | tf_op jit(solution)/shard_map/ppermute | solution.py:20
  87.7 19.0 %all-to-all-start.2 = ((bf16[16,32,512]{2,0,1:T(8,128)(2,1)}), bf16[16,32,512]{2,0,1:T(8,128)(2,1)S(1)}, u32[]{:S(2)}, u32[]{:S(2)}) async-start(bf16[16,32,512]{2,0,1:T(8,128)(2,1)} %copy.23), calls=%async_computation.2 | async-start | bytes 1048576 | tf_op jit(solution)/shard_map/all_to_all | solution.py:60
Sparse Core Ops, SparseCore 0:
  37.2 58.3 all-gather.1
